TPU v7x, 32 devices: a whole 2x2x4 slice. The times are simulated.
32 devices in a mesh: row: 16 (over z, x, core), col: 2 (over y).
Axes of the slice: x: 2, y: 2, z: 4, core: 2. Of those that a mesh axis runs over, the one named last changes fastest.
Arguments:
- counts: int32 [3072, 3072], P('row', 'col'), may hold values from 0 to 3
- theta: bfloat16 [3072, 64], P(('row', 'col')), may hold values from 0.099609375 to 1
- phi: bfloat16 [3072, 64], P(('col', 'row')), may hold values from 0.099609375 to 1
- affinity: float32 [64, 64], replicated, may hold values from 0.0003 to 0.003
Outputs:
- theta_grad: float32 [3072, 64], P(('row', 'col'))
- phi_grad: float32 [3072, 64], P(('col', 'row'))
- affinity_grad: float32 [64, 64], replicated
All inputs are finite; a program needn't handle non-finite values.
Results may differ from a plain program's by a relative error of at most 0.0003.
Values may be sent and summed in bfloat16 or wider, within the bound.
No kernel may reach another device: no remote copies, remote signals or barrier semaphores. Data moves between devices by JAX's collectives and lax.ppermute only.
A program may use at most 64 MiB of HBM per device.

v0:
```python
import jax
import jax.numpy as jnp
from jax import lax
from jax.sharding import PartitionSpec as P


def shards(counts, theta, phi, affinity):
    nodes = theta.shape[0] * lax.axis_size("row") * lax.axis_size("col")
    inverse = 1.0 / nodes
    theta_rows = lax.all_gather(theta, "col", axis=0, tiled=True)
    row_factor = jnp.dot(theta_rows.astype(jnp.float32), affinity, precision=lax.Precision.HIGHEST)
    factor_half = row_factor.astype(jnp.bfloat16)
    members = lax.all_gather(phi, "row", axis=0, tiled=True)
    rate = jnp.dot(row_factor, members.astype(jnp.float32).T, precision=lax.Precision.HIGHEST)
    ratio = (1.0 - counts.astype(jnp.float32) / rate).astype(jnp.bfloat16)
    gphi = jnp.dot(ratio, members, preferred_element_type=jnp.float32)
    phi_sum = lax.psum_scatter(
        lax.dot_general(
            ratio, factor_half, (((0,), (0,)), ((), ())), preferred_element_type=jnp.float32
        ),
        "row",
        scatter_dimension=0,
        tiled=True,
    )
    gphi_sum = lax.psum_scatter(gphi, "col", scatter_dimension=0, tiled=True)
    theta_grad = inverse * jnp.dot(gphi_sum, affinity.T, precision=lax.Precision.HIGHEST)
    phi_grad = inverse * phi_sum
    affinity_part = jnp.dot(theta.astype(jnp.float32).T, gphi_sum, precision=lax.Precision.HIGHEST)
    affinity_grad = inverse * inverse * lax.psum(affinity_part, ("row", "col"))
    return (theta_grad, phi_grad, affinity_grad)


def solution(mesh):
    placed = (P("row", "col"), P(("row", "col"), None), P(("col", "row"), None), P())
    return jax.shard_map(
        shards,
        mesh=mesh,
        in_specs=placed,
        out_specs=(P(("row", "col"), None), P(("col", "row"), None), P()),
        check_vma=False,
    )
```

profile of v0, /device:TPU:0, one launch (start us, length us, event | category | flops | bytes accessed | tf_op | source)
XLA Modules:
  0.0 114.5 jit_solution(16224483972441247521)
XLA Ops:
  7.2 0.0 copy-start
  7.2 0.0 copy-start.2
  7.2 0.0 reduce-scatter.7.cloned.1.call-start
  7.2 5.7 %all-gather = bf16[2,96,64]{1,2,0:T(8,128)(2,1)S(1)} all-gather(bf16[1,96,64]{1,2,0:T(8,128)(2,1)} %bitcast.21), channel_id=1, replica_groups=mesh['row'=16,'col'=2] {'col'}, dimensions={0}, use_global_device_ids=true | all-gather | bytes 36864 | tf_op jit(solution)/shard_map/all_gather | solution.py:10
  13.0 0.1 reshape.7
  13.1 23.0 %all-gather.1 = bf16[16,96,64]{1,2,0:T(8,128)(2,1)S(1)} all-gather(bf16[1,96,64]{1,2,0:T(8,128)(2,1)} %bitcast.22), channel_id=1, replica_groups=mesh['row'=16,'col'=2] {'row'}, dimensions={0}, use_global_device_ids=true | all-gather | bytes 208896 | tf_op jit(solution)/shard_map/all_gather | solution.py:13
  36.2 0.2 copy.12
  36.3 0.3 reshape.9
  36.6 0.0 copy-done
  36.6 0.2 fusion.4
  36.8 0.0 copy-done.2
  36.8 0.7 fusion.1
  37.6 0.9 fusion.5
  38.5 0.0 copy-start.1
  38.5 0.0 reduce-scatter.7.cloned.1.call-update
  38.6 0.0 reduce-scatter.9.cloned.1.call-start
  38.6 1.3 %fusion.2 = f32[1536,64]{1,0:T(8,128)} fusion(bf16[192,1536]{1,0:T(8,128)(2,1)S(1)} %fusion.1, f32[192,64]{0,1:T(8,128)S(1)} %fusion.4), kind=kOutput, calls=%fused_computation.5 | convolution fusion | flops 37761024 | bytes 1032192
  39.9 0.0 reduce-scatter.9.cloned.1.call-update
  40.0 6.1 %reduce-scatter.7.cloned.1.call-done = f32[96,64]{1,0:T(8,128)} async-done(((f32[192,64]{1,0:T(8,128)}), f32[96,64]{1,0:T(8,128)}) %reduce-scatter.7.cloned.1.call-update) | async-done | bytes 24592
  46.0 0.0 copy-done.1
  46.0 1.0 convolution_bitcast_fusion
  47.0 39.5 %psum.7 = f32[64,64]{0,1:T(8,128)S(1)} all-reduce(f32[64,64]{0,1:T(8,128)S(1)} %convolution_bitcast_fusion), channel_id=1, replica_groups=mesh['row'=16,'col'=2] {'row','col'}, use_global_device_ids=true, to_apply=%region_2.0 | all-reduce | flops 4096 | bytes 32768 | tf_op jit(solution)/shard_map/psum | solution.py:29
  86.6 0.7 copy.13
  87.3 1.6 %convolution_multiply_fusion = f32[96,64]{0,1:T(8,128)} fusion(f32[96,64]{1,0:T(8,128)} %reduce-scatter.7.cloned.1.call-done, f32[64,64]{1,0:T(8,128)S(1)} %copy-done), kind=kOutput, calls=%fused_computation.4 | convolution fusion | flops 4724736 | bytes 65536 | tf_op jit(solution)/shard_map/dot_general | solution.py:26
  88.9 17.3 %reduce-scatter.9.cloned.1.call-done = f32[96,64]{1,0:T(8,128)} async-done(((f32[1536,64]{1,0:T(8,128)}), f32[96,64]{1,0:T(8,128)}) %reduce-scatter.9.cloned.1.call-update) | async-done | bytes 24592
  106.2 0.9 copy.17
  107.0 0.6 broadcast_multiply_fusion.1
  (2 shorter events, 0.0 us)
Async XLA Ops:
  7.2 29.4 %copy-start = (f32[64,64]{1,0:T(8,128)S(1)}, f32[64,64]{1,0:T(8,128)}, u32[]{:S(2)}) copy-start(f32[64,64]{1,0:T(8,128)} %param.7) | copy-start | bytes 49156
  7.2 29.7 %copy-start.2 = (s32[192,1536]{1,0:T(8,128)S(1)}, s32[192,1536]{1,0:T(8,128)}, u32[]{:S(2)}) copy-start(s32[192,1536]{1,0:T(8,128)} %param.4) | copy-start | bytes 3538948
  7.2 38.8 %reduce-scatter.7.cloned.1.call-start = ((), (), s32[]{:S(2)}) async-start(), calls=%async_computation.2 | async-start | bytes 147456
  38.5 7.5 %copy-start.1 = (bf16[96,64]{0,1:T(8,128)(2,1)S(1)}, bf16[96,64]{0,1:T(8,128)(2,1)}, u32[]{:S(2)}) copy-start(bf16[96,64]{0,1:T(8,128)(2,1)} %param.5) | copy-start | bytes 36868
  38.6 67.6 %reduce-scatter.9.cloned.1.call-start = ((), (), s32[]{:S(2)}) async-start(), calls=%async_computation.3 | async-start | bytes 835584
Sparse Core Ops, SparseCore 0:
  38.7 7.2 reduce-scatter.6
  49.6 56.5 reduce-scatter.8
where the time goes:
time: 115 us; the launch traced here: 114 us
  blocking collectives  68.3 us (59%)
  waiting for transfers between devices  23.3 us (20%)
  between operations  14.1 us (12%)
  matrix products  5.89 us (5%)
  local copies, waits for them, and re-layouts  2.15 us (2%)
    psum x1, blocking collectives, shards(): affinity_grad = inverse * inverse * lax.psum(affinity_part, ('row', 'col'))  39.5 us
    unnamed x4, waiting for transfers between devices  23.3 us
    all_gather x1, blocking collectives, shards(): members = lax.all_gather(phi, 'row', axis=0, tiled=True)  23 us
    all_gather x1, blocking collectives, shards(): theta_rows = lax.all_gather(theta, 'col', axis=0, tiled=True)  5.75 us
  transfers between devices with their start and end apart: 2, of which 2 were waited for; matrix products, arithmetic and copies ran while one was open for 4% of the time, Pallas kernels for 0%

commit v1 on v0

--- a/solution.py
+++ b/solution.py
@@ -26,7 +26,9 @@
     theta_grad = inverse * jnp.dot(gphi_sum, affinity.T, precision=lax.Precision.HIGHEST)
     phi_grad = inverse * phi_sum
     affinity_part = jnp.dot(theta.astype(jnp.float32).T, gphi_sum, precision=lax.Precision.HIGHEST)
-    affinity_grad = inverse * inverse * lax.psum(affinity_part, ("row", "col"))
+    affinity_grad = (
+        inverse * inverse * jnp.sum(lax.all_gather(affinity_part, ("row", "col")), axis=0)
+    )
     return (theta_grad, phi_grad, affinity_grad)
 
 

time: 115 us -> 131 us (1.14)
  blocking collectives: 68.3 us -> 102 us
  waiting for transfers between devices: 23.3 us -> 6.09 us
    all_gather x0 -> x1, blocking collectives: none -> 73.3 us  [shards(): lax.all_gather(affinity_part, ('row', 'col'))]
    psum x1 -> x0, blocking collectives: 39.5 us -> none  [shards(): affinity_grad = inverse * inverse * lax.psum(affinity_part, ('row', 'col'))]
    unnamed x4, waiting for transfers between devices: 23.3 us -> 6.09 us
  transfers between devices with their start and end apart: 2 -> 2, of which waited for: 2 -> 1; matrix products, arithmetic and copies ran while one was open for 4% -> 3% of each run, Pallas kernels for 0% -> 0%
where the time goes in v1:
time: 131 us; the launch traced here: 130 us
  blocking collectives  102 us (78%)
  between operations  14.1 us (11%)
  waiting for transfers between devices  6.09 us (5%)
  matrix products  5.09 us (4%)
  local copies, waits for them, and re-layouts  2.3 us (2%)
    all_gather x1, blocking collectives, shards(): lax.all_gather(affinity_part, ('row', 'col'))  73.3 us
    all_gather x1, blocking collectives, shards(): members = lax.all_gather(phi, 'row', axis=0, tiled=True)  23 us
    unnamed x4, waiting for transfers between devices  6.09 us
    all_gather x1, blocking collectives, shards(): theta_rows = lax.all_gather(theta, 'col', axis=0, tiled=True)  5.75 us
  transfers between devices with their start and end apart: 2, of which 1 were waited for; matrix products, arithmetic and copies ran while one was open for 3% of the time, Pallas kernels for 0%

profile of v1, /device:TPU:0, one launch (start us, length us, event | category | flops | bytes accessed | tf_op | source)
XLA Modules:
  0.0 130.4 jit_solution(4352712040459780495)
XLA Ops:
  7.2 0.0 copy-start
  7.2 0.0 copy-start.3
  7.2 0.0 reduce-scatter.7.cloned.1.call-start
  7.2 5.7 %all-gather.1 = bf16[2,96,64]{1,2,0:T(8,128)(2,1)S(1)} all-gather(bf16[1,96,64]{1,2,0:T(8,128)(2,1)} %bitcast.23), channel_id=1, replica_groups=mesh['row'=16,'col'=2] {'col'}, dimensions={0}, use_global_device_ids=true | all-gather | bytes 36864 | tf_op jit(solution)/shard_map/all_gather | solution.py:10
  13.0 0.1 reshape.8
  13.1 23.0 %all-gather.2 = bf16[16,96,64]{1,2,0:T(8,128)(2,1)S(1)} all-gather(bf16[1,96,64]{1,2,0:T(8,128)(2,1)} %bitcast.24), channel_id=1, replica_groups=mesh['row'=16,'col'=2] {'row'}, dimensions={0}, use_global_device_ids=true | all-gather | bytes 208896 | tf_op jit(solution)/shard_map/all_gather | solution.py:13
  36.2 0.2 copy.10
  36.3 0.3 reshape.10
  36.6 0.0 copy-done
  36.6 0.2 fusion.4
  36.8 0.0 copy-done.3
  36.8 0.7 fusion.1
  37.6 0.9 fusion.5
  38.5 0.0 copy-start.2
  38.5 0.0 reduce-scatter.7.cloned.1.call-update
  38.6 0.0 reduce-scatter.9.cloned.1.call-start
  38.6 1.3 %fusion.2 = f32[1536,64]{1,0:T(8,128)} fusion(bf16[192,1536]{1,0:T(8,128)(2,1)S(1)} %fusion.1, f32[192,64]{0,1:T(8,128)S(1)} %fusion.4), kind=kOutput, calls=%fused_computation.5 | convolution fusion | flops 37761024 | bytes 1032192
  39.9 0.0 reduce-scatter.9.cloned.1.call-update
  40.0 6.1 %reduce-scatter.7.cloned.1.call-done = f32[96,64]{1,0:T(8,128)} async-done(((f32[192,64]{1,0:T(8,128)}), f32[96,64]{1,0:T(8,128)}) %reduce-scatter.7.cloned.1.call-update) | async-done | bytes 24592
  46.0 0.0 copy-done.2
  46.0 1.0 convolution_bitcast_fusion
  47.0 0.1 copy.11
  47.1 0.0 copy-start.1
  47.1 73.3 %all-gather = f32[2048,64]{1,0:T(8,128)S(1)} all-gather(f32[64,64]{1,0:T(8,128)S(1)} %copy.11), channel_id=2, replica_groups=mesh['row'=16,'col'=2] {'row','col'}, dimensions={0}, use_global_device_ids=true | all-gather | bytes 540672 | tf_op jit(solution)/shard_map/all_gather | solution.py:30
  120.4 0.1 reduce_sum.9
  120.5 0.1 copy.18
  120.6 0.7 copy.13
  121.3 0.0 copy-done.1
  121.3 0.8 convolution_multiply_fusion
  122.1 0.0 reduce-scatter.9.cloned.1.call-done
  122.1 0.9 copy.17
  123.0 0.6 broadcast_multiply_fusion.1
  (2 shorter events, 0.0 us)
Async XLA Ops:
  7.2 29.4 %copy-start = (f32[64,64]{1,0:T(8,128)S(1)}, f32[64,64]{1,0:T(8,128)}, u32[]{:S(2)}) copy-start(f32[64,64]{1,0:T(8,128)} %param.7) | copy-start | bytes 49156
  7.2 29.7 %copy-start.3 = (s32[192,1536]{1,0:T(8,128)S(1)}, s32[192,1536]{1,0:T(8,128)}, u32[]{:S(2)}) copy-start(s32[192,1536]{1,0:T(8,128)} %param.4) | copy-start | bytes 3538948
  7.2 38.8 %reduce-scatter.7.cloned.1.call-start = ((), (), s32[]{:S(2)}) async-start(), calls=%async_computation.2 | async-start | bytes 147456
  38.5 7.5 %copy-start.2 = (bf16[96,64]{0,1:T(8,128)(2,1)S(1)}, bf16[96,64]{0,1:T(8,128)(2,1)}, u32[]{:S(2)}) copy-start(bf16[96,64]{0,1:T(8,128)(2,1)} %param.5) | copy-start | bytes 36868
  38.6 83.5 %reduce-scatter.9.cloned.1.call-start = ((), (), s32[]{:S(2)}) async-start(), calls=%async_computation.3 | async-start | bytes 835584
  47.1 74.1 %copy-start.1 = (f32[96,64]{1,0:T(8,128)S(1)}, f32[96,64]{1,0:T(8,128)}, u32[]{:S(2)}) copy-start(f32[96,64]{1,0:T(8,128)} %reduce-scatter.7.cloned.1.call-done) | copy-start | bytes 73732
Sparse Core Ops, SparseCore 0:
  38.7 7.2 reduce-scatter.6
  49.6 56.7 reduce-scatter.8
